TPU v7x, 128 devices: a whole 4x4x4 slice. The times are simulated.
128 devices in a mesh: sample: 32 (over x, y, core), protein: 4 (over z).
Axes of the slice: x: 4, y: 4, z: 4, core: 2. Of those that a mesh axis runs over, the one named last changes fastest.
Arguments:
- proteins: bfloat16 [16384, 2048], P('sample'), may hold values from -34 to 34
- dosage: bfloat16 [16384, 2048], P('sample'), may hold values from 0 to 2, as said below
Outputs:
- scores: float32 [2048, 2048], P('sample', 'protein')
Inputs may be any that keep to these rules, and one draw needn't show every extreme that they name: `dosage`: allele dosages, whole numbers.
All inputs are finite; a program needn't handle non-finite values.
Results may differ from a plain program's by a relative error of at most 0.0003.
Values sent between devices are 32-bit elements; how exact they have to be, the bound alone decides.
No kernel may reach another device: no remote copies, remote signals or barrier semaphores. Data moves between devices by JAX's collectives and lax.ppermute only.
A program may use at most 128 MiB of HBM per device.

v0:
```python
import math

import jax
import jax.numpy as jnp
from jax import lax
from jax.sharding import PartitionSpec as P


def side_by_side(arrays, axis, dim, along):
    widths = [math.prod(a.shape[along:]) for a in arrays]
    both = jnp.concatenate(
        [a.reshape(*a.shape[:along], w) for a, w in zip(arrays, widths)], axis=along
    )
    filled = lax.psum_scatter(both, axis, scatter_dimension=dim, tiled=True)
    tiles = jnp.split(filled, [sum(widths[:k]) for k in range(1, len(widths))], axis=along)
    return tuple(
        (b.reshape(*filled.shape[:along], *a.shape[along:]) for a, b in zip(arrays, tiles))
    )


def from_root(value, axis, root):
    return lax.dynamic_index_in_dim(lax.all_gather(value, axis), root, 0, keepdims=False)


def right_solve(factor, rows):
    return jax.scipy.linalg.solve_triangular(factor, rows.T, lower=True).T


def split_cholesky(matrix):
    order = matrix.shape[0]
    if order <= 128 or order % 2 != 0:
        return jnp.linalg.cholesky(matrix)
    half = order // 2
    leading = split_cholesky(matrix[:half, :half])
    below = right_solve(leading, matrix[half:, :half])
    trailing = matrix[half:, half:] - jnp.dot(below, below.T, precision=lax.Precision.HIGHEST)
    trailing_factor = split_cholesky(trailing)
    upper_rows = jnp.concatenate([leading, jnp.zeros((half, order - half), jnp.float32)], 1)
    lower_rows = jnp.concatenate([below, trailing_factor], 1)
    return jnp.concatenate([upper_rows, lower_rows], 0)


def body(proteins, dosage):
    total_proteins = proteins.shape[1]
    groups = lax.axis_size("protein")
    block_width = total_proteins // groups
    column = lax.axis_index("protein")
    sample_count = proteins.shape[0] * lax.axis_size("sample")
    contract = (((0,), (0,)), ((), ()))
    own_proteins = lax.dynamic_slice_in_dim(proteins, column * block_width, block_width, 1)
    gram_part = lax.dot_general(
        proteins, own_proteins, contract, preferred_element_type=jnp.float32
    )
    cross_part = lax.dot_general(dosage, own_proteins, contract, preferred_element_type=jnp.float32)
    protein_sums = jnp.sum(own_proteins, axis=0, dtype=jnp.float32)
    dose_sums = jnp.sum(dosage, axis=0, dtype=jnp.float32)
    dose_squares = jnp.sum(dosage * dosage, axis=0, dtype=jnp.float32)
    gram_total, protein_sums = lax.psum((gram_part, protein_sums), "sample")
    cross, dose_sums, dose_squares = side_by_side(
        (cross_part, dose_sums, dose_squares), "sample", 0, 1
    )
    gram = gram_total / sample_count
    means = dose_sums / sample_count
    spread = jnp.sqrt(dose_squares / sample_count - means * means + 1e-05)
    centred = (cross - means[:, None] * protein_sums[None, :]) / (
        spread[:, None] * math.sqrt(sample_count)
    )
    working = gram
    diagonal_block = jnp.zeros((block_width, block_width), jnp.float32)
    row_blocks = []
    for section in range(groups):
        current = working[section * block_width : (section + 1) * block_width]
        section_factor = split_cholesky(current)
        diagonal_block = jnp.where(column == section, section_factor, diagonal_block)
        if section < groups - 1:
            lower_rows = working[(section + 1) * block_width :]
            panel_own = right_solve(section_factor, lower_rows)
            panel = from_root(panel_own, "protein", section)
            relative = jnp.clip(column - section - 1, 0, groups - section - 2)
            my_block = lax.dynamic_slice_in_dim(panel, relative * block_width, block_width, 0)
            my_block = jnp.where(column > section, my_block, jnp.zeros_like(my_block))
            row_blocks.append(my_block)
            update = jnp.dot(panel, my_block.T, precision=lax.Precision.HIGHEST)
            working = working.at[(section + 1) * block_width :].add(-update)
    remaining = centred
    for section in range(groups - 1):
        finished = right_solve(diagonal_block, remaining)
        solved_block = from_root(finished, "protein", section)
        remaining = remaining - jnp.dot(
            solved_block, row_blocks[section].T, precision=lax.Precision.HIGHEST
        )
    scores = right_solve(diagonal_block, remaining)
    return scores


def solution(mesh):
    in_specs = (P("sample", None), P("sample", None))
    out_specs = P("sample", "protein")
    return jax.shard_map(body, mesh=mesh, in_specs=in_specs, out_specs=out_specs, check_vma=False)
```

profile of v0, /device:TPU:0, one launch (start us, length us, event | category | flops | bytes accessed | tf_op | source)
XLA Modules:
  0.0 1187.5 jit_solution(13768140101091617105)
XLA Ops:
  11.7 113.8 %all-reduce.14.cloned.1.call-done = f32[2048,512]{0,1:T(8,128)} async-done(((f32[2048,512]{0,1:T(8,128)}), f32[2048,512]{0,1:T(8,128)}) %all-reduce.14.cloned.1.call-update) | async-done | bytes 4194320 | tf_op jit(solution)/shard_map/psum | solution.py:58
  130.9 11.7 cholesky.254
  157.2 11.7 cholesky.265
  174.9 19.7 %custom-call.40 = f32[2,128,128]{1,2,0:T(8,128)S(1)} custom-call(f32[2,128,128]{2,1,0:T(8,128)S(1)} %get-tuple-element.121), custom_call_target="InvertDiagBlocksLowerTriangular" | custom-call | tf_op jit(solution)/shard_map/jit(_solve_triangular)/triangular_solve | solution.py:26
  197.3 11.7 cholesky.276
  224.8 11.7 cholesky.287
  246.5 39.5 %custom-call.23 = f32[4,128,128]{1,2,0:T(8,128)S(1)} custom-call(f32[4,128,128]{2,1,0:T(8,128)S(1)} %get-tuple-element.68), custom_call_target="InvertDiagBlocksLowerTriangular" | custom-call | tf_op jit(solution)/shard_map/jit(_solve_triangular)/triangular_solve | solution.py:26
  304.0 118.1 %all-gather.10.cloned.1.call-done = f32[6144,512]{1,0:T(8,128)} async-done(((f32[1536,512]{1,0:T(8,128)}), f32[6144,512]{1,0:T(8,128)}) %all-gather.10.cloned.1.call-update) | async-done | bytes 12582928 | tf_op jit(solution)/shard_map/all_gather | solution.py:22
  455.2 11.9 cholesky.309
  473.4 20.3 %custom-call.43 = f32[2,128,128]{1,2,0:T(8,128)} custom-call(f32[2,128,128]{2,1,0:T(8,128)S(1)} %get-tuple-element.122), custom_call_target="InvertDiagBlocksLowerTriangular" | custom-call | tf_op jit(solution)/shard_map/jit(_solve_triangular)/triangular_solve | solution.py:26
  536.1 13.2 %cholesky.331 = f32[128,128]{1,0:T(8,128)} custom-call(f32[128,128]{1,0:T(8,128)} %fusion.188), custom_call_target="Cholesky" | custom-call | tf_op jit(solution)/shard_map/jit(cholesky)/cholesky | solution.py:32
  553.6 12.0 %while.23 = (s32[]{:T(128)}, f32[512,512]{1,0:T(8,128)}, s32[4,2]{0,1:T(2,128)S(1)}, f32[4,128,128]{2,1,0:T(8,128)S(1)}, s32[]{:T(128)}) while((s32[]{:T(128)}, f32[512,512]{1,0:T(8,128)}, s32[4,2]{0,1:T(2,128)S(1)}, f32[4,128,128]{2,1,0:T(8,128)S(1)}, s32[]{:T(128)}) %tuple.193), condition=%wide.while_cond.6, body=%wide.while_body.6.sunk | while | flops 2 | bytes 131181 | solution.py:26
  566.3 40.5 %custom-call.24 = f32[4,128,128]{1,2,0:T(8,128)S(1)} custom-call(f32[4,128,128]{2,1,0:T(8,128)} %copy-done.35), custom_call_target="InvertDiagBlocksLowerTriangular" | custom-call | tf_op jit(solution)/shard_map/jit(_solve_triangular)/triangular_solve | solution.py:26
  642.3 70.3 %all-gather.12.cloned.1.call-done = f32[4096,512]{1,0:T(8,128)} async-done(((f32[1024,512]{1,0:T(8,128)}), f32[4096,512]{1,0:T(8,128)}) %all-gather.12.cloned.1.call-update) | async-done | bytes 8388624 | tf_op jit(solution)/shard_map/all_gather | solution.py:22
  747.0 12.1 %cholesky.353 = f32[128,128]{1,0:T(8,128)S(1)} custom-call(f32[128,128]{1,0:T(8,128)S(1)} %fusion.185), custom_call_target="Cholesky" | custom-call | tf_op jit(solution)/shard_map/jit(cholesky)/cholesky | solution.py:32
  764.7 19.7 %custom-call.46 = f32[2,128,128]{1,2,0:T(8,128)S(1)} custom-call(f32[2,128,128]{2,1,0:T(8,128)S(1)} %get-tuple-element.123), custom_call_target="InvertDiagBlocksLowerTriangular" | custom-call | tf_op jit(solution)/shard_map/jit(_solve_triangular)/triangular_solve | solution.py:26
  837.0 40.9 %custom-call.25 = f32[4,128,128]{1,2,0:T(8,128)} custom-call(f32[4,128,128]{2,1,0:T(8,128)} %get-tuple-element.84), custom_call_target="InvertDiagBlocksLowerTriangular" | custom-call | tf_op jit(solution)/shard_map/jit(_solve_triangular)/triangular_solve | solution.py:26
  896.9 66.8 %psum.15 = f32[512]{0:T(512)S(1)} all-reduce(f32[512]{0:T(512)S(1)} %convert_reduce_fusion.2), channel_id=1, replica_groups=mesh['sample'=32,'protein'=4] {'sample'}, use_global_device_ids=true, to_apply=%region_7.11 | all-reduce | flops 512 | bytes 4096 | tf_op jit(solution)/shard_map/psum | solution.py:58
  993.7 12.1 %cholesky.397 = f32[128,128]{1,0:T(8,128)S(1)} custom-call(f32[128,128]{1,0:T(8,128)S(1)} %fusion.179), custom_call_target="Cholesky" | custom-call | tf_op jit(solution)/shard_map/jit(cholesky)/cholesky | solution.py:32
  1013.2 19.7 %custom-call.49 = f32[2,128,128]{1,2,0:T(8,128)S(1)} custom-call(f32[2,128,128]{2,1,0:T(8,128)S(1)} %get-tuple-element.124), custom_call_target="InvertDiagBlocksLowerTriangular" | custom-call | tf_op jit(solution)/shard_map/jit(_solve_triangular)/triangular_solve | solution.py:26
  1085.2 40.3 %custom-call.54 = f32[4,128,128]{1,2,0:T(8,128)S(1)} custom-call(f32[4,128,128]{2,1,0:T(8,128)} %copy-done.34), custom_call_target="InvertDiagBlocksLowerTriangular" | custom-call | tf_op jit(solution)/shard_map/jit(_solve_triangular)/triangular_solve | solution.py:26
  1130.2 13.2 %all-gather.3 = f32[256,512]{1,0:T(8,128)S(1)} all-gather(f32[64,512]{1,0:T(8,128)S(1)} %maximum_bitcast_fusion.3), channel_id=5, replica_groups=mesh['sample'=32,'protein'=4] {'protein'}, dimensions={0}, use_global_device_ids=true | all-gather | bytes 655360 | tf_op jit(solution)/shard_map/all_gather | solution.py:22
  1147.4 13.2 %all-gather.4 = f32[256,512]{1,0:T(8,128)S(1)} all-gather(f32[64,512]{1,0:T(8,128)S(1)} %maximum_bitcast_fusion.4), channel_id=6, replica_groups=mesh['sample'=32,'protein'=4] {'protein'}, dimensions={0}, use_global_device_ids=true | all-gather | bytes 655360 | tf_op jit(solution)/shard_map/all_gather | solution.py:22
  1163.3 12.8 %all-gather.5 = f32[256,512]{1,0:T(8,128)S(1)} all-gather(f32[64,512]{1,0:T(8,128)S(1)} %maximum_bitcast_fusion.5), channel_id=7, replica_groups=mesh['sample'=32,'protein'=4] {'protein'}, dimensions={0}, use_global_device_ids=true | all-gather | bytes 655360 | tf_op jit(solution)/shard_map/all_gather | solution.py:22
  (431 shorter events, 471.9 us)
Async XLA Ops:
  6.5 118.9 %all-reduce.14.cloned.1.call-start = ((), (), s32[]{:S(2)}) async-start(), calls=%async_computation.1 | async-start | bytes 8388608 | tf_op jit(solution)/shard_map/psum | solution.py:58
  11.6 410.5 %all-gather.10.cloned.1.call-start = ((), (), s32[]{:S(2)}) async-start(), calls=%async_computation.2 | async-start | bytes 15728640 | tf_op jit(solution)/shard_map/all_gather | solution.py:22
  170.3 67.7 %copy-start.19 = (f32[256,256]{1,0:T(8,128)}, f32[256,256]{1,0:T(8,128)S(1)}, u32[]{:S(2)}) copy-start(f32[256,256]{1,0:T(8,128)S(1)} %get-tuple-element.233) | copy-start | bytes 786436
  195.7 42.3 %copy-start.13 = (f32[256,256]{1,0:T(8,128)}, f32[256,256]{1,0:T(8,128)S(1)}, u32[]{:S(2)}) copy-start(f32[256,256]{1,0:T(8,128)S(1)} %fusion.89) | copy-start | bytes 786436
  210.3 27.6 %copy-start.25 = (f32[128,128]{1,0:T(8,128)}, f32[128,128]{1,0:T(8,128)S(1)}, u32[]{:S(2)}) copy-start(f32[128,128]{1,0:T(8,128)S(1)} %get-tuple-element.208) | copy-start | bytes 196612
  220.8 17.1 %copy-start.28 = (f32[128,128]{0,1:T(8,128)}, f32[128,128]{0,1:T(8,128)S(1)}, u32[]{:S(2)}) copy-start(f32[128,128]{0,1:T(8,128)S(1)} %copy.73) | copy-start | bytes 196612
  237.9 8.5 copy-start.29
  303.5 409.1 %all-gather.12.cloned.1.call-start = ((), (), s32[]{:S(2)}) async-start(), calls=%async_computation.3 | async-start | bytes 10485760 | tf_op jit(solution)/shard_map/all_gather | solution.py:22
  499.7 51.7 %copy-start.15 = (f32[256,256]{1,0:T(8,128)}, f32[256,256]{1,0:T(8,128)S(1)}, u32[]{:S(2)}) copy-start(f32[256,256]{1,0:T(8,128)S(1)} %fusion.88) | copy-start | bytes 786436
  531.5 20.0 %copy-start.30 = (f32[128,128]{0,1:T(8,128)S(1)}, f32[128,128]{0,1:T(8,128)}, u32[]{:S(2)}) copy-start(f32[128,128]{0,1:T(8,128)} %copy.89) | copy-start | bytes 196612
  628.2 335.4 %reduce-scatter.4.cloned.1.call-start = ((), (), s32[]{:S(2)}) async-start(), calls=%async_computation.5 | async-start | bytes 5406720 | tf_op jit(solution)/shard_map/reduce_scatter | solution.py:14
  642.1 324.3 %all-gather.14.cloned.1.call-start = ((), (), s32[]{:S(2)}) async-start(), calls=%async_computation.4 | async-start | bytes 5242880 | tf_op jit(solution)/shard_map/all_gather | solution.py:22
  719.4 66.0 %copy-start.7 = (f32[1024,512]{0,1:T(8,128)S(1)}, f32[1024,512]{0,1:T(8,128)}, u32[]{:S(2)}) copy-start(f32[1024,512]{0,1:T(8,128)} %copy-done.6) | copy-start | bytes 6291460
  760.6 64.0 %copy-start.22 = (f32[256,256]{1,0:T(8,128)}, f32[256,256]{1,0:T(8,128)S(1)}, u32[]{:S(2)}) copy-start(f32[256,256]{1,0:T(8,128)S(1)} %get-tuple-element.229) | copy-start | bytes 786436
  764.7 59.9 %copy-start.37 = (s32[2,2]{1,0:T(2,128)}, s32[2,2]{1,0:T(2,128)S(1)}, u32[]{:S(2)}) copy-start(s32[2,2]{1,0:T(2,128)S(1)} %get-tuple-element.624) | copy-start | bytes 52
  799.1 78.8 %copy-start.27 = (f32[128,128]{1,0:T(8,128)}, f32[128,128]{1,0:T(8,128)S(1)}, u32[]{:S(2)}) copy-start(f32[128,128]{1,0:T(8,128)S(1)} %get-tuple-element.200) | copy-start | bytes 196612
  1007.2 66.1 %copy-start.14 = (f32[256,256]{1,0:T(8,128)S(1)}, f32[256,256]{1,0:T(8,128)}, u32[]{:S(2)}) copy-start(f32[256,256]{1,0:T(8,128)} %copy-done.13) | copy-start | bytes 786436
  1007.2 66.1 %copy-start.16 = (f32[256,256]{1,0:T(8,128)S(1)}, f32[256,256]{1,0:T(8,128)}, u32[]{:S(2)}) copy-start(f32[256,256]{1,0:T(8,128)} %copy-done.15) | copy-start | bytes 786436
  1007.2 66.1 %copy-start.18 = (f32[256,256]{1,0:T(8,128)S(1)}, f32[256,256]{1,0:T(8,128)}, u32[]{:S(2)}) copy-start(f32[256,256]{1,0:T(8,128)} %copy-done.17) | copy-start | bytes 786436
  1007.2 66.1 %copy-start.20 = (f32[256,256]{1,0:T(8,128)S(1)}, f32[256,256]{1,0:T(8,128)}, u32[]{:S(2)}) copy-start(f32[256,256]{1,0:T(8,128)} %copy-done.19) | copy-start | bytes 786436
  1007.2 66.1 %copy-start.21 = (f32[256,256]{1,0:T(8,128)S(1)}, f32[256,256]{1,0:T(8,128)}, u32[]{:S(2)}) copy-start(f32[256,256]{1,0:T(8,128)} %get-tuple-element.231) | copy-start | bytes 786436
  1007.2 66.1 %copy-start.23 = (f32[256,256]{1,0:T(8,128)S(1)}, f32[256,256]{1,0:T(8,128)}, u32[]{:S(2)}) copy-start(f32[256,256]{1,0:T(8,128)} %copy-done.22) | copy-start | bytes 786436
  1007.2 66.1 %copy-start.26 = (f32[128,128]{1,0:T(8,128)S(1)}, f32[128,128]{1,0:T(8,128)}, u32[]{:S(2)}) copy-start(f32[128,128]{1,0:T(8,128)} %copy-done.25) | copy-start | bytes 196612
  1085.2 75.4 %copy-start.3 = (f32[1024,512]{1,0:T(8,128)S(1)}, f32[1024,512]{1,0:T(8,128)}, u32[]{:S(2)}) copy-start(f32[1024,512]{1,0:T(8,128)} %copy-done.2) | copy-start | bytes 6291460
  (19 other events, 44.4 us)
Sparse Core Ops, SparseCore 0:
  11.7 113.6 all-reduce.13
  303.7 118.4 all-gather.9
  628.3 84.2 all-gather.11
  716.2 85.6 reduce-scatter.3
  895.8 49.1 all-gather.13
where the time goes:
time: 1200 us; the launch traced here: 1190 us
  other arithmetic  565 us (47%)
  waiting for transfers between devices  302 us (25%)
  blocking collectives  106 us (9%)
  local copies, waits for them, and re-layouts  102 us (8%)
  matrix products  95.4 us (8%)
  between operations  15.3 us (1%)
    another operation x30, other arithmetic, right_solve(): return jax.scipy.linalg.solve_triangular(factor, rows.T, lower=True).T  332 us
    another operation x48, other arithmetic, split_cholesky(): return jnp.linalg.cholesky(matrix)  202 us
    all_gather x3, waiting for transfers between devices, from_root(): lax.all_gather(value, axis)  188 us
    psum x1, waiting for transfers between devices, body(): gram_total, protein_sums = lax.psum((gram_part, protein_sums), 'sample')  114 us
    psum x1, blocking collectives, body(): gram_total, protein_sums = lax.psum((gram_part, protein_sums), 'sample')  66.8 us
    another operation x69, matrix products, right_solve(): return jax.scipy.linalg.solve_triangular(factor, rows.T, lower=True).T  60.6 us
    another operation x63, local copies, waits for them, and re-layouts, right_solve(): return jax.scipy.linalg.solve_triangular(factor, rows.T, lower=True).T  40 us
    all_gather x3, blocking collectives, from_root(): lax.all_gather(value, axis)  39.1 us
  transfers between devices with their start and end apart: 5, of which 3 were waited for; matrix products, arithmetic and copies ran while one was open for 17% of the time, Pallas kernels for 0%

commit v1 on v0

v1 whole, which is shorter than its diff:
```python
import functools
import math

import jax
import jax.numpy as jnp
from jax import lax
from jax.experimental import pallas as pl
from jax.experimental.pallas import tpu as pltpu
from jax.sharding import PartitionSpec as P

BLOCK = 128
CHUNK = 256
HIGHEST = lax.Precision.HIGHEST


def side_by_side(arrays, axis, dim, along):
    widths = [math.prod(a.shape[along:]) for a in arrays]
    both = jnp.concatenate(
        [a.reshape(*a.shape[:along], w) for a, w in zip(arrays, widths)], axis=along
    )
    filled = lax.psum_scatter(both, axis, scatter_dimension=dim, tiled=True)
    tiles = jnp.split(filled, [sum(widths[:k]) for k in range(1, len(widths))], axis=along)
    return tuple(
        (b.reshape(*filled.shape[:along], *a.shape[along:]) for a, b in zip(arrays, tiles))
    )


def dot_t(a, b):
    return lax.dot_general(
        a, b, (((1,), (1,)), ((), ())), precision=HIGHEST, preferred_element_type=jnp.float32
    )


def inverse_factor(block):
    b = block.shape[0]
    rio = lax.broadcasted_iota(jnp.int32, (b, b), 0)
    lio = lax.broadcasted_iota(jnp.int32, (b, b), 1)
    rcol = lax.broadcasted_iota(jnp.int32, (b, 1), 0)
    lrow = lax.broadcasted_iota(jnp.int32, (1, b), 1)

    def step(j, m):
        row = jnp.sum(jnp.where(rio == j, m, 0.0), axis=0, keepdims=True)
        pivot = jnp.sum(jnp.where(lrow == j, row, 0.0), axis=1, keepdims=True)
        scale = lax.rsqrt(pivot)
        new_row = jnp.where(lrow == j, scale, row * scale)
        col = jnp.sum(jnp.where(lio == j, m, 0.0), axis=1, keepdims=True)
        mult = jnp.where(rcol > j, col * scale, 0.0)
        m = jnp.where((rio > j) & (lio == j), 0.0, m) - mult * new_row
        return jnp.where(rio == j, jnp.where(lrow <= j, new_row, 0.0), m)

    return lax.fori_loop(0, b, step, block)


def factor_solve_kernel(g_hbm, c_ref, out_ref, g_ref, sem):
    n = g_ref.shape[0]
    b = BLOCK
    copy = pltpu.make_async_copy(g_hbm, g_ref, sem)
    copy.start()
    out_ref[...] = c_ref[...]
    copy.wait()
    for k in range(n // b):
        r0 = k * b
        inv = inverse_factor(g_ref[r0 : r0 + b, r0 : r0 + b])
        solved = dot_t(out_ref[:, r0 : r0 + b], inv)
        out_ref[:, r0 : r0 + b] = solved
        rest = r0 + b
        if rest < n:
            panel = dot_t(g_ref[rest:, r0 : r0 + b], inv)
            for a in range(rest, n, CHUNK):
                e = min(a + CHUNK, n)
                g_ref[a:e, rest:] = g_ref[a:e, rest:] - dot_t(panel[a - rest : e - rest], panel)
            out_ref[:, rest:] = out_ref[:, rest:] - dot_t(solved, panel)


def factor_solve(gram, rows):
    n = gram.shape[0]
    return pl.pallas_call(
        factor_solve_kernel,
        out_shape=jax.ShapeDtypeStruct(rows.shape, jnp.float32),
        in_specs=[
            pl.BlockSpec(memory_space=pl.ANY),
            pl.BlockSpec(memory_space=pltpu.VMEM),
        ],
        out_specs=pl.BlockSpec(memory_space=pltpu.VMEM),
        scratch_shapes=[pltpu.VMEM((n, n), jnp.float32), pltpu.SemaphoreType.DMA],
        compiler_params=pltpu.CompilerParams(vmem_limit_bytes=56 * 1024 * 1024),
    )(gram, rows)


def body(proteins, dosage):
    total_proteins = proteins.shape[1]
    groups = lax.axis_size("protein")
    block_width = total_proteins // groups
    column = lax.axis_index("protein")
    sample_count = proteins.shape[0] * lax.axis_size("sample")
    contract = (((0,), (0,)), ((), ()))
    own_proteins = lax.dynamic_slice_in_dim(proteins, column * block_width, block_width, 1)
    gram_part = lax.dot_general(
        proteins, own_proteins, contract, preferred_element_type=jnp.float32
    )
    cross_part = lax.dot_general(dosage, own_proteins, contract, preferred_element_type=jnp.float32)
    protein_sums = jnp.sum(own_proteins, axis=0, dtype=jnp.float32)
    dose_sums = jnp.sum(dosage, axis=0, dtype=jnp.float32)
    dose_squares = jnp.sum(dosage * dosage, axis=0, dtype=jnp.float32)
    gram_total, protein_sums = lax.psum((gram_part, protein_sums), "sample")
    cross, dose_sums, dose_squares = side_by_side(
        (cross_part, dose_sums, dose_squares), "sample", 0, 1
    )
    gram_cols = gram_total / sample_count
    gram = lax.all_gather(gram_cols, "protein", axis=1, tiled=True)
    means = dose_sums / sample_count
    spread = jnp.sqrt(dose_squares / sample_count - means * means + 1e-05)
    centred = (cross - means[:, None] * protein_sums[None, :]) / (
        spread[:, None] * math.sqrt(sample_count)
    )
    centred_rows = lax.all_gather(centred, "protein", axis=1, tiled=True)
    scores_rows = factor_solve(gram, centred_rows)
    return lax.dynamic_slice_in_dim(scores_rows, column * block_width, block_width, 1)


def solution(mesh):
    in_specs = (P("sample", None), P("sample", None))
    out_specs = P("sample", "protein")
    return jax.shard_map(body, mesh=mesh, in_specs=in_specs, out_specs=out_specs, check_vma=False)
```

time: 1200 us -> 737 us (0.61)
  other arithmetic: 565 us -> 11.6 us
  Pallas kernels: 0 us -> 355 us
  local copies, waits for them, and re-layouts: 102 us -> 3.4 us
  matrix products: 95.4 us -> 7.61 us
  waiting for transfers between devices: 302 us -> 260 us
  blocking collectives: 106 us -> 81.2 us
    another operation x78 -> x0, other arithmetic: 534 us -> none  [the longest x30 332 us: right_solve(): return jax.scipy.linalg.solve_triangular(factor, rows.T, lower=True).T]
    pallas_call x0 -> x1, Pallas kernels: none -> 355 us  [factor_solve(): pl.pallas_call(factor_solve_kernel, out_shape=jax.ShapeDtypeStruct(rows.s...]
    another operation x99 -> x0, local copies, waits for them, and re-layouts: 70.8 us -> none  [the longest x63 40 us: right_solve(): return jax.scipy.linalg.solve_triangular(factor, rows.T, lower=True).T]
    another operation x69 -> x0, matrix products: 60.6 us -> none  [right_solve(): return jax.scipy.linalg.solve_triangular(factor, rows.T, lower=True).T]
    all_gather x3 -> x1, waiting for transfers between devices: 188 us -> 139 us  [body(): gram = lax.all_gather(gram_cols, 'protein', axis=1, tiled=True)]
    dot_general x18 -> x0, matrix products: 27.4 us -> none  [the longest x3 12.5 us: body(): update = jnp.dot(panel, my_block.T, precision=lax.Precision.HIGHEST)]
    all_gather x3 -> x1, blocking collectives: 39.1 us -> 14.7 us  [body(): centred_rows = lax.all_gather(centred, 'protein', axis=1, tiled=True)]
    reduce_scatter x1, waiting for transfers between devices: 0.01 us -> 15.7 us  [side_by_side(): filled = lax.psum_scatter(both, axis, scatter_dimension=dim, tiled=True)]
  transfers between devices with their start and end apart: 5 -> 3, of which waited for: 3 -> 3; matrix products, arithmetic and copies ran while one was open for 17% -> 2% of each run, Pallas kernels for 0% -> 0%
where the time goes in v1:
time: 737 us; the launch traced here: 732 us
  Pallas kernels  355 us (48%)
  waiting for transfers between devices  260 us (35%)
  blocking collectives  81.2 us (11%)
  between operations  13.3 us (2%)
  other arithmetic  11.6 us (2%)
  matrix products  7.61 us (1%)
    pallas_call x1, Pallas kernels, factor_solve(): pl.pallas_call(factor_solve_kernel, out_shape=jax.ShapeDtypeStruct(rows.s...  355 us
    all_gather x1, waiting for transfers between devices, body(): gram = lax.all_gather(gram_cols, 'protein', axis=1, tiled=True)  139 us
    psum x1, waiting for transfers between devices, body(): gram_total, protein_sums = lax.psum((gram_part, protein_sums), 'sample')  106 us
    psum x1, blocking collectives, body(): gram_total, protein_sums = lax.psum((gram_part, protein_sums), 'sample')  66.6 us
    reduce_scatter x1, waiting for transfers between devices, side_by_side(): filled = lax.psum_scatter(both, axis, scatter_dimension=dim, tiled=True)  15.7 us
  transfers between devices with their start and end apart: 3, of which 3 were waited for; matrix products, arithmetic and copies ran while one was open for 2% of the time, Pallas kernels for 0%

profile of v1, /device:TPU:0, one launch (start us, length us, event | category | flops | bytes accessed | tf_op | source)
XLA Modules:
  0.0 732.1 jit_solution(5339090840460603994)
XLA Ops:
  6.5 0.0 all-reduce.2.cloned.1.call-start
  6.5 5.2 convolution_bitcast_fusion.1
  11.7 0.0 all-reduce.2.cloned.1.call-update
  11.7 0.0 reduce-scatter.2.cloned.1.call-start
  11.8 0.0 copy-done
  11.8 0.7 convert_reduce_fusion.1
  12.5 0.4 copy.8
  12.8 1.5 copy.7
  14.3 2.4 convolution_bitcast_fusion
  16.7 3.0 pad_maximum_fusion
  19.8 0.0 reduce-scatter.2.cloned.1.call-update
  19.8 0.0 all-gather.2.cloned.1.call-start
  19.8 105.8 %all-reduce.2.cloned.1.call-done = f32[2048,512]{1,0:T(8,128)} async-done(((f32[2048,512]{1,0:T(8,128)}), f32[2048,512]{1,0:T(8,128)}) %all-reduce.2.cloned.1.call-update) | async-done | bytes 4194320 | tf_op jit(solution)/shard_map/psum | solution.py:105
  125.7 4.7 broadcast_multiply_fusion
  130.4 0.0 all-gather.2.cloned.1.call-update
  130.4 1.2 convert_reduce_fusion.2
  131.5 66.6 %psum.15 = f32[512]{0:T(512)S(1)} all-reduce(f32[512]{0:T(512)S(1)} %convert_reduce_fusion.2), channel_id=1, replica_groups=mesh['sample'=32,'protein'=4] {'sample'}, use_global_device_ids=true, to_apply=%region_5.0 | all-reduce | flops 512 | bytes 4096 | tf_op jit(solution)/shard_map/psum | solution.py:105
  198.1 15.7 %reduce-scatter.2.cloned.1.call-done = f32[64,514]{1,0:T(8,128)} async-done(((f32[2048,514]{1,0:T(8,128)}), f32[64,514]{1,0:T(8,128)}) %reduce-scatter.2.cloned.1.call-update) | async-done | bytes 131600 | tf_op jit(solution)/shard_map/reduce_scatter | solution.py:21
  213.8 1.0 fusion.8
  214.9 1.0 fusion.2
  215.9 14.7 %all_gather.7.c_ref = f32[64,2048]{1,0:T(8,128)} all-gather(f32[64,512]{1,0:T(8,128)S(1)} %fusion.2), channel_id=1, replica_groups=mesh['sample'=32,'protein'=4] {'protein'}, dimensions={1}, use_global_device_ids=true | all-gather | bytes 655360 | tf_op jit(solution)/shard_map/all_gather | solution.py:116
  230.5 138.5 %all-gather.2.cloned.1.call-done.g_hbm = f32[2048,2048]{1,0:T(8,128)} async-done(((f32[2048,512]{1,0:T(8,128)}), f32[2048,2048]{1,0:T(8,128)}) %all-gather.2.cloned.1.call-update) | async-done | bytes 16777232 | tf_op jit(solution)/shard_map/all_gather | solution.py:110
  369.1 354.8 %shard_map.28 = f32[64,2048]{1,0:T(8,128)} custom-call(f32[2048,2048]{1,0:T(8,128)} %all-gather.2.cloned.1.call-done.g_hbm, f32[64,2048]{1,0:T(8,128)} %all_gather.7.c_ref), custom_call_target="tpu_custom_call" | custom-call | tf_op jit(solution)/shard_map/pallas_call | solution.py:77
  723.8 1.6 constant_dynamic-slice_fusion
  (3 shorter events, 0.0 us)
Async XLA Ops:
  6.5 119.1 %all-reduce.2.cloned.1.call-start = ((), (), s32[]{:S(2)}) async-start(), calls=%async_computation.1 | async-start | bytes 8388608 | tf_op jit(solution)/shard_map/psum | solution.py:105
  6.5 5.3 copy-start
  11.7 202.1 %reduce-scatter.2.cloned.1.call-start = ((), (), s32[]{:S(2)}) async-start(), calls=%async_computation.3 | async-start | bytes 5406720 | tf_op jit(solution)/shard_map/reduce_scatter | solution.py:21
  14.3 2.4 copy-start.1
  19.8 349.3 %all-gather.2.cloned.1.call-start = ((), (), s32[]{:S(2)}) async-start(), calls=%async_computation.2 | async-start | bytes 20971520 | tf_op jit(solution)/shard_map/all_gather | solution.py:110
Sparse Core Ops, SparseCore 0:
  11.9 113.7 all-reduce.1
  129.4 84.4 reduce-scatter.1
  215.5 153.5 all-gather.1

commit v2 on v1

--- a/solution.py
+++ b/solution.py
@@ -33,22 +33,27 @@
 
 def inverse_factor(block):
     b = block.shape[0]
-    rio = lax.broadcasted_iota(jnp.int32, (b, b), 0)
-    lio = lax.broadcasted_iota(jnp.int32, (b, b), 1)
-    rcol = lax.broadcasted_iota(jnp.int32, (b, 1), 0)
-    lrow = lax.broadcasted_iota(jnp.int32, (1, b), 1)
-
-    def step(j, m):
-        row = jnp.sum(jnp.where(rio == j, m, 0.0), axis=0, keepdims=True)
-        pivot = jnp.sum(jnp.where(lrow == j, row, 0.0), axis=1, keepdims=True)
-        scale = lax.rsqrt(pivot)
-        new_row = jnp.where(lrow == j, scale, row * scale)
-        col = jnp.sum(jnp.where(lio == j, m, 0.0), axis=1, keepdims=True)
-        mult = jnp.where(rcol > j, col * scale, 0.0)
-        m = jnp.where((rio > j) & (lio == j), 0.0, m) - mult * new_row
-        return jnp.where(rio == j, jnp.where(lrow <= j, new_row, 0.0), m)
-
-    return lax.fori_loop(0, b, step, block)
+    sub = lax.broadcasted_iota(jnp.int32, (8, b), 0)
+    lane = lax.broadcasted_iota(jnp.int32, (8, b), 1)
+    lane_row = lax.broadcasted_iota(jnp.int32, (1, b), 1)
+    tiles = [block[r : r + 8, :] for r in range(0, b, 8)]
+    for j in range(b):
+        home, t = divmod(j, 8)
+        row = tiles[home][t : t + 1, :]
+        scale = lax.rsqrt(row[:, j : j + 1])
+        new_row = jnp.where(lane_row == j, scale, row * scale)
+        for r in range(home, len(tiles)):
+            tile = tiles[r]
+            mult = tile[:, j : j + 1] * scale
+            hit = lane == j
+            if r == home:
+                mult = jnp.where(sub[:, 0:1] > t, mult, 0.0)
+                hit = hit & (sub > t)
+            tile = jnp.where(hit, 0.0, tile) - mult * new_row
+            if r == home:
+                tile = jnp.where(sub == t, jnp.where(lane_row <= j, new_row, 0.0), tile)
+            tiles[r] = tile
+    return jnp.concatenate(tiles, axis=0)
 
 
 def factor_solve_kernel(g_hbm, c_ref, out_ref, g_ref, sem):
@@ -82,7 +87,10 @@
             pl.BlockSpec(memory_space=pltpu.VMEM),
         ],
         out_specs=pl.BlockSpec(memory_space=pltpu.VMEM),
-        scratch_shapes=[pltpu.VMEM((n, n), jnp.float32), pltpu.SemaphoreType.DMA],
+        scratch_shapes=[
+            pltpu.VMEM((n, n), jnp.float32),
+            pltpu.SemaphoreType.DMA,
+        ],
         compiler_params=pltpu.CompilerParams(vmem_limit_bytes=56 * 1024 * 1024),
     )(gram, rows)
 

time: 737 us -> 589 us (0.80)
  Pallas kernels: 355 us -> 207 us
    pallas_call x1, Pallas kernels: 355 us -> 207 us  [factor_solve(): pl.pallas_call(factor_solve_kernel, out_shape=jax.ShapeDtypeStruct(rows.s...]
  transfers between devices with their start and end apart: 3 -> 3, of which waited for: 3 -> 3; matrix products, arithmetic and copies ran while one was open for 2% -> 3% of each run, Pallas kernels for 0% -> 0%
where the time goes in v2:
time: 589 us; the launch traced here: 584 us
  waiting for transfers between devices  260 us (44%)
  Pallas kernels  207 us (35%)
  blocking collectives  81.4 us (14%)
  between operations  13.3 us (2%)
  other arithmetic  11.6 us (2%)
  matrix products  7.61 us (1%)
    pallas_call x1, Pallas kernels, factor_solve(): pl.pallas_call(factor_solve_kernel, out_shape=jax.ShapeDtypeStruct(rows.s...  207 us
    all_gather x1, waiting for transfers between devices, body(): gram = lax.all_gather(gram_cols, 'protein', axis=1, tiled=True)  138 us
    psum x1, waiting for transfers between devices, body(): gram_total, protein_sums = lax.psum((gram_part, protein_sums), 'sample')  106 us
    psum x1, blocking collectives, body(): gram_total, protein_sums = lax.psum((gram_part, protein_sums), 'sample')  66.6 us
    reduce_scatter x1, waiting for transfers between devices, side_by_side(): filled = lax.psum_scatter(both, axis, scatter_dimension=dim, tiled=True)  15.7 us
    all_gather x1, blocking collectives, body(): centred_rows = lax.all_gather(centred, 'protein', axis=1, tiled=True)  14.8 us
  transfers between devices with their start and end apart: 3, of which 3 were waited for; matrix products, arithmetic and copies ran while one was open for 3% of the time, Pallas kernels for 0%

profile of v2, /device:TPU:0, one launch (start us, length us, event | category | flops | bytes accessed | tf_op | source)
XLA Modules:
  0.0 583.9 jit_solution(18444578435291320716)
XLA Ops:
  6.5 0.0 all-reduce.2.cloned.1.call-start
  6.5 5.2 convolution_bitcast_fusion.1
  11.7 0.0 all-reduce.2.cloned.1.call-update
  11.7 0.0 reduce-scatter.2.cloned.1.call-start
  11.8 0.0 copy-done
  11.8 0.7 convert_reduce_fusion.1
  12.5 0.4 copy.8
  12.8 1.5 copy.7
  14.3 2.4 convolution_bitcast_fusion
  16.7 3.0 pad_maximum_fusion
  19.8 0.0 reduce-scatter.2.cloned.1.call-update
  19.8 0.0 all-gather.2.cloned.1.call-start
  19.8 105.8 %all-reduce.2.cloned.1.call-done = f32[2048,512]{1,0:T(8,128)} async-done(((f32[2048,512]{1,0:T(8,128)}), f32[2048,512]{1,0:T(8,128)}) %all-reduce.2.cloned.1.call-update) | async-done | bytes 4194320 | tf_op jit(solution)/shard_map/psum | solution.py:113
  125.7 4.7 broadcast_multiply_fusion
  130.4 0.0 all-gather.2.cloned.1.call-update
  130.4 1.2 convert_reduce_fusion.2
  131.6 66.6 %psum.15 = f32[512]{0:T(512)S(1)} all-reduce(f32[512]{0:T(512)S(1)} %convert_reduce_fusion.2), channel_id=1, replica_groups=mesh['sample'=32,'protein'=4] {'sample'}, use_global_device_ids=true, to_apply=%region_5.0 | all-reduce | flops 512 | bytes 4096 | tf_op jit(solution)/shard_map/psum | solution.py:113
  198.1 15.7 %reduce-scatter.2.cloned.1.call-done = f32[64,514]{1,0:T(8,128)} async-done(((f32[2048,514]{1,0:T(8,128)}), f32[64,514]{1,0:T(8,128)}) %reduce-scatter.2.cloned.1.call-update) | async-done | bytes 131600 | tf_op jit(solution)/shard_map/reduce_scatter | solution.py:21
  213.8 1.0 fusion.8
  214.9 1.0 fusion.2
  215.9 14.8 %all_gather.7.c_ref = f32[64,2048]{1,0:T(8,128)} all-gather(f32[64,512]{1,0:T(8,128)S(1)} %fusion.2), channel_id=1, replica_groups=mesh['sample'=32,'protein'=4] {'protein'}, dimensions={1}, use_global_device_ids=true | all-gather | bytes 655360 | tf_op jit(solution)/shard_map/all_gather | solution.py:124
  230.7 138.3 %all-gather.2.cloned.1.call-done.g_hbm = f32[2048,2048]{1,0:T(8,128)} async-done(((f32[2048,512]{1,0:T(8,128)}), f32[2048,2048]{1,0:T(8,128)}) %all-gather.2.cloned.1.call-update) | async-done | bytes 16777232 | tf_op jit(solution)/shard_map/all_gather | solution.py:118
  369.1 206.6 %shard_map.28 = f32[64,2048]{1,0:T(8,128)} custom-call(f32[2048,2048]{1,0:T(8,128)} %all-gather.2.cloned.1.call-done.g_hbm, f32[64,2048]{1,0:T(8,128)} %all_gather.7.c_ref), custom_call_target="tpu_custom_call" | custom-call | tf_op jit(solution)/shard_map/pallas_call | solution.py:82
  575.6 1.6 constant_dynamic-slice_fusion
  (3 shorter events, 0.0 us)
Async XLA Ops:
  6.5 119.1 %all-reduce.2.cloned.1.call-start = ((), (), s32[]{:S(2)}) async-start(), calls=%async_computation.1 | async-start | bytes 8388608 | tf_op jit(solution)/shard_map/psum | solution.py:113
  6.5 5.3 copy-start
  11.7 202.1 %reduce-scatter.2.cloned.1.call-start = ((), (), s32[]{:S(2)}) async-start(), calls=%async_computation.3 | async-start | bytes 5406720 | tf_op jit(solution)/shard_map/reduce_scatter | solution.py:21
  14.3 2.4 copy-start.1
  19.8 349.3 %all-gather.2.cloned.1.call-start = ((), (), s32[]{:S(2)}) async-start(), calls=%async_computation.2 | async-start | bytes 20971520 | tf_op jit(solution)/shard_map/all_gather | solution.py:118
Sparse Core Ops, SparseCore 0:
  11.9 113.7 all-reduce.1
  129.4 84.4 reduce-scatter.1
  215.5 153.5 all-gather.1

commit v3 on v2

--- a/solution.py
+++ b/solution.py
@@ -1,4 +1,3 @@
-import functools
 import math
 
 import jax
@@ -56,43 +55,70 @@
     return jnp.concatenate(tiles, axis=0)
 
 
-def factor_solve_kernel(g_hbm, c_ref, out_ref, g_ref, sem):
+def factor_kernel(g_hbm, l_hbm, g_ref, sem):
     n = g_ref.shape[0]
     b = BLOCK
     copy = pltpu.make_async_copy(g_hbm, g_ref, sem)
+    copy.start()
+    copy.wait()
+    for k in range(n // b):
+        r0 = k * b
+        inv = inverse_factor(g_ref[r0 : r0 + b, r0 : r0 + b])
+        g_ref[r0 : r0 + b, r0 : r0 + b] = inv
+        rest = r0 + b
+        if rest < n:
+            panel = dot_t(g_ref[rest:, r0 : r0 + b], inv)
+            g_ref[rest:, r0 : r0 + b] = panel
+            for a in range(rest, n, CHUNK):
+                e = min(a + CHUNK, n)
+                g_ref[a:e, rest:] = g_ref[a:e, rest:] - dot_t(panel[a - rest : e - rest], panel)
+    copy = pltpu.make_async_copy(g_ref, l_hbm, sem)
+    copy.start()
+    copy.wait()
+
+
+def solve_kernel(l_hbm, c_ref, out_ref, l_ref, sem):
+    n = l_ref.shape[0]
+    b = BLOCK
+    copy = pltpu.make_async_copy(l_hbm, l_ref, sem)
     copy.start()
     out_ref[...] = c_ref[...]
     copy.wait()
     for k in range(n // b):
         r0 = k * b
-        inv = inverse_factor(g_ref[r0 : r0 + b, r0 : r0 + b])
-        solved = dot_t(out_ref[:, r0 : r0 + b], inv)
+        solved = dot_t(out_ref[:, r0 : r0 + b], l_ref[r0 : r0 + b, r0 : r0 + b])
         out_ref[:, r0 : r0 + b] = solved
         rest = r0 + b
         if rest < n:
-            panel = dot_t(g_ref[rest:, r0 : r0 + b], inv)
-            for a in range(rest, n, CHUNK):
-                e = min(a + CHUNK, n)
-                g_ref[a:e, rest:] = g_ref[a:e, rest:] - dot_t(panel[a - rest : e - rest], panel)
-            out_ref[:, rest:] = out_ref[:, rest:] - dot_t(solved, panel)
+            out_ref[:, rest:] = out_ref[:, rest:] - dot_t(solved, l_ref[rest:, r0 : r0 + b])
 
 
-def factor_solve(gram, rows):
+def factor(gram):
     n = gram.shape[0]
     return pl.pallas_call(
-        factor_solve_kernel,
+        factor_kernel,
+        out_shape=jax.ShapeDtypeStruct(gram.shape, jnp.float32),
+        in_specs=[pl.BlockSpec(memory_space=pl.ANY)],
+        out_specs=pl.BlockSpec(memory_space=pl.ANY),
+        scratch_shapes=[pltpu.VMEM((n, n), jnp.float32), pltpu.SemaphoreType.DMA],
+        input_output_aliases={0: 0},
+        compiler_params=pltpu.CompilerParams(vmem_limit_bytes=56 * 1024 * 1024),
+    )(gram)
+
+
+def solve(factored, rows):
+    n = factored.shape[0]
+    return pl.pallas_call(
+        solve_kernel,
         out_shape=jax.ShapeDtypeStruct(rows.shape, jnp.float32),
         in_specs=[
             pl.BlockSpec(memory_space=pl.ANY),
             pl.BlockSpec(memory_space=pltpu.VMEM),
         ],
         out_specs=pl.BlockSpec(memory_space=pltpu.VMEM),
-        scratch_shapes=[
-            pltpu.VMEM((n, n), jnp.float32),
-            pltpu.SemaphoreType.DMA,
-        ],
-        compiler_params=pltpu.CompilerParams(vmem_limit_bytes=56 * 1024 * 1024),
-    )(gram, rows)
+        scratch_shapes=[pltpu.VMEM((n, n), jnp.float32), pltpu.SemaphoreType.DMA],
+        compiler_params=pltpu.CompilerParams(vmem_limit_bytes=40 * 1024 * 1024),
+    )(factored, rows)
 
 
 def body(proteins, dosage):
@@ -110,19 +136,27 @@
     protein_sums = jnp.sum(own_proteins, axis=0, dtype=jnp.float32)
     dose_sums = jnp.sum(dosage, axis=0, dtype=jnp.float32)
     dose_squares = jnp.sum(dosage * dosage, axis=0, dtype=jnp.float32)
-    gram_total, protein_sums = lax.psum((gram_part, protein_sums), "sample")
+    stacked = jnp.concatenate(
+        [gram_part, protein_sums[None, :], jnp.zeros((7, block_width), jnp.float32)], axis=0
+    )
+    stacked = lax.psum(stacked, "sample")
+    gram_cols = stacked[:total_proteins] / sample_count
+    protein_sums = stacked[total_proteins]
+    gram = lax.all_gather(gram_cols, "protein", axis=1, tiled=True)
+    gram, cross_part, dose_sums, dose_squares = lax.optimization_barrier(
+        (gram, cross_part, dose_sums, dose_squares)
+    )
+    factored = factor(gram)
     cross, dose_sums, dose_squares = side_by_side(
         (cross_part, dose_sums, dose_squares), "sample", 0, 1
     )
-    gram_cols = gram_total / sample_count
-    gram = lax.all_gather(gram_cols, "protein", axis=1, tiled=True)
     means = dose_sums / sample_count
     spread = jnp.sqrt(dose_squares / sample_count - means * means + 1e-05)
     centred = (cross - means[:, None] * protein_sums[None, :]) / (
         spread[:, None] * math.sqrt(sample_count)
     )
     centred_rows = lax.all_gather(centred, "protein", axis=1, tiled=True)
-    scores_rows = factor_solve(gram, centred_rows)
+    scores_rows = solve(factored, centred_rows)
     return lax.dynamic_slice_in_dim(scores_rows, column * block_width, block_width, 1)
 
 

time: 589 us -> 563 us (0.956)
  blocking collectives: 81.4 us -> 13.6 us
  Pallas kernels: 207 us -> 227 us
  local copies, waits for them, and re-layouts: 3.4 us -> 13.7 us
    psum x1 -> x0, blocking collectives: 66.6 us -> none  [body(): gram_total, protein_sums = lax.psum((gram_part, protein_sums), 'sample')]
    pallas_call x1 -> x2, Pallas kernels: 207 us -> 227 us  [the longest x1 208 us: factor(): pl.pallas_call(factor_kernel, out_shape=jax.ShapeDtypeStruct(gram.shape,...]
    reduce_scatter x1, waiting for transfers between devices: 15.7 us -> 0.02 us  [side_by_side(): filled = lax.psum_scatter(both, axis, scatter_dimension=dim, tiled=True)]
    concatenate x0 -> x1, local copies, waits for them, and re-layouts: none -> 10.7 us  [body(): jnp.concatenate([gram_part, protein_sums[None, :], jnp.zeros((7, block_wi...]
    all_gather x1, waiting for transfers between devices: 138 us -> 147 us  [body(): gram = lax.all_gather(gram_cols, 'protein', axis=1, tiled=True)]
    psum x1, waiting for transfers between devices: 106 us -> 114 us  [body(): stacked = lax.psum(stacked, 'sample')]
  transfers between devices with their start and end apart: 3 -> 3, of which waited for: 3 -> 2; matrix products, arithmetic and copies ran while one was open for 3% -> 1% of each run, Pallas kernels for 0% -> 38%
where the time goes in v3:
time: 563 us; the launch traced here: 553 us
  waiting for transfers between devices  261 us (46%)
  Pallas kernels  227 us (40%)
  other arithmetic  13.7 us (2%)
  local copies, waits for them, and re-layouts  13.7 us (2%)
  blocking collectives  13.6 us (2%)
  between operations  13.6 us (2%)
  matrix products  9.45 us (2%)
    pallas_call x1, Pallas kernels, factor(): pl.pallas_call(factor_kernel, out_shape=jax.ShapeDtypeStruct(gram.shape,...  208 us
    all_gather x1, waiting for transfers between devices, body(): gram = lax.all_gather(gram_cols, 'protein', axis=1, tiled=True)  147 us
    psum x1, waiting for transfers between devices, body(): stacked = lax.psum(stacked, 'sample')  114 us
    pallas_call x1, Pallas kernels, solve(): pl.pallas_call(solve_kernel, out_shape=jax.ShapeDtypeStruct(rows.shape, j...  19.3 us
    all_gather x1, blocking collectives, body(): centred_rows = lax.all_gather(centred, 'protein', axis=1, tiled=True)  13.6 us
  transfers between devices with their start and end apart: 3, of which 2 were waited for; matrix products, arithmetic and copies ran while one was open for 1% of the time, Pallas kernels for 38%

profile of v3, /device:TPU:0, one launch (start us, length us, event | category | flops | bytes accessed | tf_op | source)
XLA Modules:
  0.0 552.7 jit_solution(1718727800527223453)
XLA Ops:
  6.5 5.0 convolution_bitcast_fusion.1
  11.6 1.2 convert_reduce_fusion.2
  12.7 10.7 %concatenate.6 = f32[2056,512]{1,0:T(8,128)} concatenate(f32[2048,512]{1,0:T(8,128)} %convolution_bitcast_fusion.1, f32[1,512]{1,0:T(1,128)S(1)} %bitcast.13, f32[7,512]{1,0:T(8,128)S(1)} %broadcast_in_dim.9), dimensions={0} | concatenate | bytes 8421376 | tf_op jit(solution)/shard_map/concatenate | solution.py:139
  23.5 0.0 all-reduce.2.cloned.1.call-update
  23.5 0.0 all-gather.2.cloned.1.call-start
  23.5 113.7 %all-reduce.2.cloned.1.call-done = f32[2056,512]{1,0:T(8,128)} async-done(((f32[2056,512]{1,0:T(8,128)}), f32[2056,512]{1,0:T(8,128)}) %all-reduce.2.cloned.1.call-update) | async-done | bytes 4210704 | tf_op jit(solution)/shard_map/psum | solution.py:142
  137.3 4.6 slice_multiply_fusion
  141.9 0.0 all-gather.2.cloned.1.call-update
  141.9 0.0 reduce-scatter.2.cloned.1.call-start
  142.0 1.5 copy-done
  143.5 0.7 convert_reduce_fusion
  144.2 4.4 convolution_bitcast_fusion
  148.6 147.4 %all-gather.2.cloned.1.call-done.g_hbm = f32[2048,2048]{1,0:T(8,128)} async-done(((f32[2048,512]{1,0:T(8,128)}), f32[2048,2048]{1,0:T(8,128)}) %all-gather.2.cloned.1.call-update) | async-done | bytes 16777232 | tf_op jit(solution)/shard_map/all_gather | solution.py:145
  296.0 0.4 copy.8
  296.4 0.4 copy.9
  296.7 5.2 pad_maximum_fusion
  301.9 0.0 reduce-scatter.2.cloned.1.call-update
  302.0 208.2 %shard_map.28.l_hbm = f32[2048,2048]{1,0:T(8,128)} custom-call(f32[2048,2048]{1,0:T(8,128)} %all-gather.2.cloned.1.call-done.g_hbm), custom_call_target="tpu_custom_call", output_to_operand_aliasing={{}: (0, {})} | custom-call | tf_op jit(solution)/shard_map/pallas_call | solution.py:98
  510.2 0.0 reduce-scatter.2.cloned.1.call-done
  510.2 1.0 fusion.8
  511.3 1.0 fusion.2
  512.3 13.6 %all_gather.7.c_ref = f32[64,2048]{1,0:T(8,128)S(1)} all-gather(f32[64,512]{1,0:T(8,128)S(1)} %fusion.2), channel_id=1, replica_groups=mesh['sample'=32,'protein'=4] {'protein'}, dimensions={1}, use_global_device_ids=true | all-gather | bytes 655360 | tf_op jit(solution)/shard_map/all_gather | solution.py:158
  525.9 19.3 %shard_map.29 = f32[64,2048]{1,0:T(8,128)S(1)} custom-call(f32[2048,2048]{1,0:T(8,128)} %shard_map.28.l_hbm, f32[64,2048]{1,0:T(8,128)S(1)} %all_gather.7.c_ref), custom_call_target="tpu_custom_call" | custom-call | tf_op jit(solution)/shard_map/pallas_call | solution.py:111
  545.2 0.7 constant_dynamic-slice_fusion
  (5 shorter events, 0.0 us)
Async XLA Ops:
  6.5 130.7 %all-reduce.2.cloned.1.call-start = ((), (), s32[]{:S(2)}) async-start(), calls=%async_computation.1 | async-start | bytes 8421376 | tf_op jit(solution)/shard_map/psum | solution.py:142
  23.5 272.5 %all-gather.2.cloned.1.call-start = ((), (), s32[]{:S(2)}) async-start(), calls=%async_computation.2 | async-start | bytes 20971520 | tf_op jit(solution)/shard_map/all_gather | solution.py:145
  141.9 1.6 copy-start
  141.9 368.3 %reduce-scatter.2.cloned.1.call-start = ((), (), s32[]{:S(2)}) async-start(), calls=%async_computation.3 | async-start | bytes 5406720 | tf_op jit(solution)/shard_map/reduce_scatter | solution.py:20
  302.0 209.3 %slice-start = ((f32[2056,512]{1,0:T(8,128)}), f32[1,512]{1,0:T(1,128)S(1)}, s32[]{:S(2)}) async-start(f32[2056,512]{1,0:T(8,128)} %all-reduce.2.cloned.1.call-done), calls=%async_computation.4 | async-start | bytes 4096 | tf_op jit(solution)/shard_map/slice | solution.py:144
Sparse Core Ops, SparseCore 0:
  23.6 113.6 all-reduce.1
  142.0 153.8 all-gather.1
  302.1 85.6 reduce-scatter.1

commit v4 on v3

--- a/solution.py
+++ b/solution.py
@@ -8,7 +8,7 @@
 from jax.sharding import PartitionSpec as P
 
 BLOCK = 128
-CHUNK = 256
+PIECE = 256
 HIGHEST = lax.Precision.HIGHEST
 
 
@@ -55,12 +55,28 @@
     return jnp.concatenate(tiles, axis=0)
 
 
-def factor_kernel(g_hbm, l_hbm, g_ref, sem):
+def lower_blocks(n, groups):
+    count = n // PIECE
+    blocks = [(i, j) for i in range(count) for j in range(i + 1)]
+    assert len(blocks) % groups == 0
+    return blocks
+
+
+def factor_kernel(packed_hbm, l_hbm, g_ref, sems):
     n = g_ref.shape[0]
     b = BLOCK
-    copy = pltpu.make_async_copy(g_hbm, g_ref, sem)
-    copy.start()
-    copy.wait()
+    blocks = lower_blocks(n, 1)
+    copies = []
+    for q, (i, j) in enumerate(blocks):
+        copy = pltpu.make_async_copy(
+            packed_hbm.at[q],
+            g_ref.at[pl.ds(i * PIECE, PIECE), pl.ds(j * PIECE, PIECE)],
+            sems.at[q],
+        )
+        copy.start()
+        copies.append(copy)
+    for copy in copies:
+        copy.wait()
     for k in range(n // b):
         r0 = k * b
         inv = inverse_factor(g_ref[r0 : r0 + b, r0 : r0 + b])
@@ -69,10 +85,12 @@
         if rest < n:
             panel = dot_t(g_ref[rest:, r0 : r0 + b], inv)
             g_ref[rest:, r0 : r0 + b] = panel
-            for a in range(rest, n, CHUNK):
-                e = min(a + CHUNK, n)
-                g_ref[a:e, rest:] = g_ref[a:e, rest:] - dot_t(panel[a - rest : e - rest], panel)
-    copy = pltpu.make_async_copy(g_ref, l_hbm, sem)
+            edges = sorted(set([rest] + list(range(-(-rest // PIECE) * PIECE, n, PIECE)) + [n]))
+            for a, e in zip(edges[:-1], edges[1:]):
+                g_ref[a:e, rest:e] = g_ref[a:e, rest:e] - dot_t(
+                    panel[a - rest : e - rest], panel[: e - rest]
+                )
+    copy = pltpu.make_async_copy(g_ref, l_hbm, sems.at[0])
     copy.start()
     copy.wait()
 
@@ -93,17 +111,18 @@
             out_ref[:, rest:] = out_ref[:, rest:] - dot_t(solved, l_ref[rest:, r0 : r0 + b])
 
 
-def factor(gram):
-    n = gram.shape[0]
+def factor(packed, n):
     return pl.pallas_call(
         factor_kernel,
-        out_shape=jax.ShapeDtypeStruct(gram.shape, jnp.float32),
+        out_shape=jax.ShapeDtypeStruct((n, n), jnp.float32),
         in_specs=[pl.BlockSpec(memory_space=pl.ANY)],
         out_specs=pl.BlockSpec(memory_space=pl.ANY),
-        scratch_shapes=[pltpu.VMEM((n, n), jnp.float32), pltpu.SemaphoreType.DMA],
-        input_output_aliases={0: 0},
+        scratch_shapes=[
+            pltpu.VMEM((n, n), jnp.float32),
+            pltpu.SemaphoreType.DMA((packed.shape[0],)),
+        ],
         compiler_params=pltpu.CompilerParams(vmem_limit_bytes=56 * 1024 * 1024),
-    )(gram)
+    )(packed)
 
 
 def solve(factored, rows):
@@ -129,24 +148,29 @@
     sample_count = proteins.shape[0] * lax.axis_size("sample")
     contract = (((0,), (0,)), ((), ()))
     own_proteins = lax.dynamic_slice_in_dim(proteins, column * block_width, block_width, 1)
+    blocks = lower_blocks(total_proteins, groups)
+    share = len(blocks) // groups
+    table = jnp.asarray([[blocks[z * share + t] for t in range(share)] for z in range(groups)], jnp.int32)
+    mine = table[column]
+    pieces = proteins.reshape(proteins.shape[0], total_proteins // PIECE, PIECE)
+    left = jnp.take(pieces, mine[:, 0], axis=1)
+    right = jnp.take(pieces, mine[:, 1], axis=1)
     gram_part = lax.dot_general(
-        proteins, own_proteins, contract, preferred_element_type=jnp.float32
+        left, right, (((0,), (0,)), ((1,), (1,))), preferred_element_type=jnp.float32
     )
     cross_part = lax.dot_general(dosage, own_proteins, contract, preferred_element_type=jnp.float32)
     protein_sums = jnp.sum(own_proteins, axis=0, dtype=jnp.float32)
     dose_sums = jnp.sum(dosage, axis=0, dtype=jnp.float32)
     dose_squares = jnp.sum(dosage * dosage, axis=0, dtype=jnp.float32)
-    stacked = jnp.concatenate(
-        [gram_part, protein_sums[None, :], jnp.zeros((7, block_width), jnp.float32)], axis=0
+    stacked = jnp.concatenate([gram_part.reshape(-1), protein_sums])
+    stacked = lax.psum(stacked, "sample")
+    gram_own = stacked[: gram_part.size].reshape(gram_part.shape) / sample_count
+    protein_sums = stacked[gram_part.size :]
+    packed = lax.all_gather(gram_own, "protein", axis=0, tiled=True)
+    packed, cross_part, dose_sums, dose_squares = lax.optimization_barrier(
+        (packed, cross_part, dose_sums, dose_squares)
     )
-    stacked = lax.psum(stacked, "sample")
-    gram_cols = stacked[:total_proteins] / sample_count
-    protein_sums = stacked[total_proteins]
-    gram = lax.all_gather(gram_cols, "protein", axis=1, tiled=True)
-    gram, cross_part, dose_sums, dose_squares = lax.optimization_barrier(
-        (gram, cross_part, dose_sums, dose_squares)
-    )
-    factored = factor(gram)
+    factored = factor(packed, total_proteins)
     cross, dose_sums, dose_squares = side_by_side(
         (cross_part, dose_sums, dose_squares), "sample", 0, 1
     )

time: 563 us -> 489 us (0.87); the launches traced: 553 us -> 485 us
  waiting for transfers between devices: 261 us -> 196 us
    all_gather x1, waiting for transfers between devices: 147 us -> 85.7 us  [body(): packed = lax.all_gather(gram_own, 'protein', axis=0, tiled=True)]
    concatenate x1 -> x0, local copies, waits for them, and re-layouts: 10.7 us -> none  [body(): jnp.concatenate([gram_part, protein_sums[None, :], jnp.zeros((7, block_wi...]
  transfers between devices with their start and end apart: 3 -> 3, of which waited for: 2 -> 2; matrix products, arithmetic and copies ran while one was open for 1% -> 1% of each run, Pallas kernels for 38% -> 42%
where the time goes in v4:
time: 489 us; the launch traced here: 485 us
  Pallas kernels  223 us (46%)
  waiting for transfers between devices  196 us (40%)
  local copies, waits for them, and re-layouts  17.7 us (4%)
  blocking collectives  13.9 us (3%)
  between operations  13.7 us (3%)
  other arithmetic  12.5 us (3%)
  matrix products  7.69 us (2%)
    pallas_call x1, Pallas kernels, factor(): pl.pallas_call(factor_kernel, out_shape=jax.ShapeDtypeStruct((n, n), jnp....  204 us
    psum x1, waiting for transfers between devices, body(): stacked = lax.psum(stacked, 'sample')  110 us
    all_gather x1, waiting for transfers between devices, body(): packed = lax.all_gather(gram_own, 'protein', axis=0, tiled=True)  85.7 us
    pallas_call x1, Pallas kernels, solve(): pl.pallas_call(solve_kernel, out_shape=jax.ShapeDtypeStruct(rows.shape, j...  19.3 us
    all_gather x1, blocking collectives, body(): centred_rows = lax.all_gather(centred, 'protein', axis=1, tiled=True)  13.9 us
  transfers between devices with their start and end apart: 3, of which 2 were waited for; matrix products, arithmetic and copies ran while one was open for 1% of the time, Pallas kernels for 42%

profile of v4, /device:TPU:0, one launch (start us, length us, event | category | flops | bytes accessed | tf_op | source)
XLA Modules:
  0.0 484.7 jit_solution(6071364671197505068)
XLA Ops:
  6.5 0.7 dynamic-slice_bitcast_fusion
  7.2 3.9 copy.16
  11.2 1.2 convert_reduce_fusion.2
  12.3 2.8 copy.17
  15.2 2.3 gather_fusion.1
  17.5 2.3 gather_fusion
  19.8 3.4 fusion
  23.2 1.2 copy.25
  24.4 1.6 pad_maximum_fusion.1
  26.0 110.4 %all-reduce.2.cloned.1.call-done = f32[590336]{0:T(1024)} async-done(((f32[590336]{0:T(1024)}), f32[590336]{0:T(1024)}) %all-reduce.2.cloned.1.call-update) | async-done | bytes 2361360 | tf_op jit(solution)/shard_map/psum | solution.py:166
  136.4 1.8 slice_multiply_fusion
  138.2 1.7 div.26
  140.2 1.3 copy-done
  141.6 0.7 convert_reduce_fusion
  142.2 4.3 convolution_bitcast_fusion
  146.5 85.7 %all-gather.2.cloned.1.call-done.packed_hbm = f32[36,256,256]{2,1,0:T(8,128)} async-done(((f32[9,256,256]{2,1,0:T(8,128)}), f32[36,256,256]{2,1,0:T(8,128)}) %all-gather.2.cloned.1.call-update) | async-done | bytes 9437200 | tf_op jit(solution)/shard_map/all_gather | solution.py:169
  232.6 0.4 copy.22
  232.9 5.3 %pad_maximum_fusion = f32[2048,514]{1,0:T(8,128)} fusion(f32[2048,1]{1,0:T(8,128)S(1)} %copy.22, f32[2048,1]{1,0:T(8,128)S(1)} %copy.21, f32[2048,512]{1,0:T(8,128)} %convolution_bitcast_fusion), kind=kLoop, calls=%fused_computation.2 | loop fusion | flops 2105344 | bytes 8421376 | tf_op jit(solution)/shard_map/concatenate | solution.py:17
  238.3 203.6 %shard_map.37.l_hbm = f32[2048,2048]{1,0:T(8,128)} custom-call(f32[36,256,256]{2,1,0:T(8,128)} %all-gather.2.cloned.1.call-done.packed_hbm), custom_call_target="tpu_custom_call" | custom-call | tf_op jit(solution)/shard_map/pallas_call | solution.py:115
  441.9 1.0 fusion.15
  442.9 1.0 fusion.9
  443.9 13.9 %all_gather.7.c_ref = f32[64,2048]{1,0:T(8,128)S(1)} all-gather(f32[64,512]{1,0:T(8,128)S(1)} %fusion.9), channel_id=1, replica_groups=mesh['sample'=32,'protein'=4] {'protein'}, dimensions={1}, use_global_device_ids=true | all-gather | bytes 655360 | tf_op jit(solution)/shard_map/all_gather | solution.py:182
  457.8 19.3 %shard_map.38 = f32[64,2048]{1,0:T(8,128)S(1)} custom-call(f32[2048,2048]{1,0:T(8,128)} %shard_map.37.l_hbm, f32[64,2048]{1,0:T(8,128)S(1)} %all_gather.7.c_ref), custom_call_target="tpu_custom_call" | custom-call | tf_op jit(solution)/shard_map/pallas_call | solution.py:130
  477.1 0.7 constant_dynamic-slice_fusion
  (13 shorter events, 0.7 us)
Async XLA Ops:
  6.5 129.9 %all-reduce.2.cloned.1.call-start = ((), (), s32[]{:S(2)}) async-start(), calls=%async_computation.1 | async-start | bytes 4726784 | tf_op jit(solution)/shard_map/psum | solution.py:166
  26.0 206.2 %all-gather.2.cloned.1.call-start = ((), (), s32[]{:S(2)}) async-start(), calls=%async_computation.2 | async-start | bytes 11796480 | tf_op jit(solution)/shard_map/all_gather | solution.py:169
  140.0 1.6 copy-start
  140.0 301.9 %reduce-scatter.2.cloned.1.call-start = ((), (), s32[]{:S(2)}) async-start(), calls=%async_computation.3 | async-start | bytes 5406720 | tf_op jit(solution)/shard_map/reduce_scatter | solution.py:20
  238.3 204.7 %slice-start = ((f32[590336]{0:T(1024)}), f32[512]{0:T(512)S(1)}, s32[]{:S(2)}) async-start(f32[590336]{0:T(1024)} %all-reduce.2.cloned.1.call-done), calls=%async_computation.4 | async-start | bytes 4096 | tf_op jit(solution)/shard_map/slice | solution.py:168
Sparse Core Ops, SparseCore 0:
  26.1 110.2 all-reduce.1
  140.1 92.0 all-gather.1
  238.4 85.6 reduce-scatter.1

commit v5 on v4

--- a/solution.py
+++ b/solution.py
@@ -100,7 +100,9 @@
     b = BLOCK
     copy = pltpu.make_async_copy(l_hbm, l_ref, sem)
     copy.start()
-    out_ref[...] = c_ref[...]
+    width = c_ref.shape[2]
+    for z in range(c_ref.shape[0]):
+        out_ref[:, z * width : (z + 1) * width] = c_ref[z]
     copy.wait()
     for k in range(n // b):
         r0 = k * b
@@ -129,7 +131,7 @@
     n = factored.shape[0]
     return pl.pallas_call(
         solve_kernel,
-        out_shape=jax.ShapeDtypeStruct(rows.shape, jnp.float32),
+        out_shape=jax.ShapeDtypeStruct((rows.shape[1], n), jnp.float32),
         in_specs=[
             pl.BlockSpec(memory_space=pl.ANY),
             pl.BlockSpec(memory_space=pltpu.VMEM),
@@ -179,7 +181,7 @@
     centred = (cross - means[:, None] * protein_sums[None, :]) / (
         spread[:, None] * math.sqrt(sample_count)
     )
-    centred_rows = lax.all_gather(centred, "protein", axis=1, tiled=True)
+    centred_rows = lax.all_gather(centred, "protein", axis=0)
     scores_rows = solve(factored, centred_rows)
     return lax.dynamic_slice_in_dim(scores_rows, column * block_width, block_width, 1)
 

time: 489 us -> 495 us (1.012)
  local copies, waits for them, and re-layouts: 17.7 us -> 24.4 us
    unnamed x4 -> x7, local copies, waits for them, and re-layouts: 6.5 us -> 13 us
where the time goes in v5:
time: 495 us; the launch traced here: 489 us
  Pallas kernels  223 us (45%)
  waiting for transfers between devices  196 us (40%)
  local copies, waits for them, and re-layouts  24.4 us (5%)
  blocking collectives  13.8 us (3%)
  between operations  13.4 us (3%)
  other arithmetic  10.9 us (2%)
  matrix products  7.72 us (2%)
    pallas_call x1, Pallas kernels, factor(): pl.pallas_call(factor_kernel, out_shape=jax.ShapeDtypeStruct((n, n), jnp....  203 us
    psum x1, waiting for transfers between devices, body(): stacked = lax.psum(stacked, 'sample')  110 us
    all_gather x1, waiting for transfers between devices, body(): packed = lax.all_gather(gram_own, 'protein', axis=0, tiled=True)  85.7 us
    pallas_call x1, Pallas kernels, solve(): pl.pallas_call(solve_kernel, out_shape=jax.ShapeDtypeStruct((rows.shape[1...  19.3 us
    all_gather x1, blocking collectives, body(): centred_rows = lax.all_gather(centred, 'protein', axis=0)  13.8 us
    unnamed x7, local copies, waits for them, and re-layouts  13 us
  transfers between devices with their start and end apart: 3, of which 2 were waited for; matrix products, arithmetic and copies ran while one was open for 1% of the time, Pallas kernels for 42%

profile of v5, /device:TPU:0, one launch (start us, length us, event | category | flops | bytes accessed | tf_op | source)
XLA Modules:
  0.0 489.2 jit_solution(4501048692985682708)
XLA Ops:
  6.5 0.7 dynamic-slice_bitcast_fusion
  7.2 3.9 copy.17
  11.2 1.2 convert_reduce_fusion.2
  12.3 2.8 copy.18
  15.2 2.3 gather_fusion.1
  17.5 2.3 gather_fusion
  19.8 3.4 fusion
  23.2 1.2 copy.27
  24.4 1.6 pad_maximum_fusion.1
  26.1 110.4 %all-reduce.2.cloned.1.call-done = f32[590336]{0:T(1024)} async-done(((f32[590336]{0:T(1024)}), f32[590336]{0:T(1024)}) %all-reduce.2.cloned.1.call-update) | async-done | bytes 2361360 | tf_op jit(solution)/shard_map/psum | solution.py:168
  136.4 1.8 slice_multiply_fusion
  138.2 1.8 div.26
  140.1 1.5 copy-done
  141.6 0.7 convert_reduce_fusion
  142.3 4.3 convolution_bitcast_fusion
  146.6 85.7 %all-gather.3.cloned.1.call-done.packed_hbm = f32[36,256,256]{2,1,0:T(8,128)} async-done(((f32[9,256,256]{2,1,0:T(8,128)}), f32[36,256,256]{2,1,0:T(8,128)}) %all-gather.3.cloned.1.call-update) | async-done | bytes 9437200 | tf_op jit(solution)/shard_map/all_gather | solution.py:171
  232.2 4.7 pad_maximum_fusion
  236.9 6.2 %copy.23 = f32[2048,514]{1,0:T(8,128)} copy(f32[2048,514]{0,1:T(8,128)} %pad_maximum_fusion) | data formatting | bytes 8421376
  243.1 203.5 %shard_map.37.l_hbm = f32[2048,2048]{1,0:T(8,128)} custom-call(f32[36,256,256]{2,1,0:T(8,128)} %all-gather.3.cloned.1.call-done.packed_hbm), custom_call_target="tpu_custom_call" | custom-call | tf_op jit(solution)/shard_map/pallas_call | solution.py:117
  446.6 0.9 fusion.12
  447.7 1.0 fusion.9
  448.7 13.8 %all-gather = f32[256,512]{1,0:T(8,128)S(1)} all-gather(f32[64,512]{1,0:T(8,128)S(1)} %fusion.9), channel_id=2, replica_groups=mesh['sample'=32,'protein'=4] {'protein'}, dimensions={0}, use_global_device_ids=true | all-gather | bytes 655360 | tf_op jit(solution)/shard_map/all_gather | solution.py:184
  462.5 19.3 %shard_map.38 = f32[64,2048]{1,0:T(8,128)S(1)} custom-call(f32[2048,2048]{1,0:T(8,128)} %shard_map.37.l_hbm, f32[4,64,512]{2,1,0:T(8,128)S(1)} %bitcast.28), custom_call_target="tpu_custom_call" | custom-call | tf_op jit(solution)/shard_map/pallas_call | solution.py:132
  481.8 0.7 constant_dynamic-slice_fusion
  (15 shorter events, 0.3 us)
Async XLA Ops:
  6.5 129.9 %all-reduce.2.cloned.1.call-start = ((), (), s32[]{:S(2)}) async-start(), calls=%async_computation.1 | async-start | bytes 4726784 | tf_op jit(solution)/shard_map/psum | solution.py:168
  26.0 206.2 %all-gather.3.cloned.1.call-start = ((), (), s32[]{:S(2)}) async-start(), calls=%async_computation.2 | async-start | bytes 11796480 | tf_op jit(solution)/shard_map/all_gather | solution.py:171
  140.0 1.6 copy-start
  140.0 306.6 %reduce-scatter.4.cloned.1.call-start = ((), (), s32[]{:S(2)}) async-start(), calls=%async_computation.3 | async-start | bytes 5406720 | tf_op jit(solution)/shard_map/reduce_scatter | solution.py:20
  243.1 204.6 %slice-start = ((f32[590336]{0:T(1024)}), f32[512]{0:T(512)S(1)}, s32[]{:S(2)}) async-start(f32[590336]{0:T(1024)} %all-reduce.2.cloned.1.call-done), calls=%async_computation.4 | async-start | bytes 4096 | tf_op jit(solution)/shard_map/slice | solution.py:170
Sparse Core Ops, SparseCore 0:
  26.1 110.2 all-reduce.1
  140.2 92.0 all-gather.2
  243.2 85.8 reduce-scatter.3

commit v6 on v4

--- a/solution.py
+++ b/solution.py
@@ -75,11 +75,13 @@
         )
         copy.start()
         copies.append(copy)
-    for copy in copies:
+    copies[0].wait()
+    first = inverse_factor(g_ref[0:b, 0:b])
+    for copy in copies[1:]:
         copy.wait()
     for k in range(n // b):
         r0 = k * b
-        inv = inverse_factor(g_ref[r0 : r0 + b, r0 : r0 + b])
+        inv = first if k == 0 else inverse_factor(g_ref[r0 : r0 + b, r0 : r0 + b])
         g_ref[r0 : r0 + b, r0 : r0 + b] = inv
         rest = r0 + b
         if rest < n:

time: 489 us -> 486 us (level)
  no operation moved by 1% of the time
where the time goes in v6:
time: 486 us; the launch traced here: 482 us
  Pallas kernels  220 us (45%)
  waiting for transfers between devices  196 us (40%)
  local copies, waits for them, and re-layouts  17.7 us (4%)
  blocking collectives  13.9 us (3%)
  between operations  13.7 us (3%)
  other arithmetic  12.5 us (3%)
  matrix products  7.69 us (2%)
    pallas_call x1, Pallas kernels, factor(): pl.pallas_call(factor_kernel, out_shape=jax.ShapeDtypeStruct((n, n), jnp....  201 us
    psum x1, waiting for transfers between devices, body(): stacked = lax.psum(stacked, 'sample')  110 us
    all_gather x1, waiting for transfers between devices, body(): packed = lax.all_gather(gram_own, 'protein', axis=0, tiled=True)  85.7 us
    pallas_call x1, Pallas kernels, solve(): pl.pallas_call(solve_kernel, out_shape=jax.ShapeDtypeStruct(rows.shape, j...  19.3 us
    all_gather x1, blocking collectives, body(): centred_rows = lax.all_gather(centred, 'protein', axis=1, tiled=True)  13.9 us
  transfers between devices with their start and end apart: 3, of which 2 were waited for; matrix products, arithmetic and copies ran while one was open for 1% of the time, Pallas kernels for 42%

profile of v6, /device:TPU:0, one launch (start us, length us, event | category | flops | bytes accessed | tf_op | source)
XLA Modules:
  0.0 482.1 jit_solution(9513912986444028719)
XLA Ops:
  6.5 0.7 dynamic-slice_bitcast_fusion
  7.2 3.9 copy.16
  11.2 1.2 convert_reduce_fusion.2
  12.3 2.8 copy.17
  15.2 2.3 gather_fusion.1
  17.5 2.3 gather_fusion
  19.8 3.4 fusion
  23.2 1.2 copy.25
  24.4 1.6 pad_maximum_fusion.1
  26.0 110.4 %all-reduce.2.cloned.1.call-done = f32[590336]{0:T(1024)} async-done(((f32[590336]{0:T(1024)}), f32[590336]{0:T(1024)}) %all-reduce.2.cloned.1.call-update) | async-done | bytes 2361360 | tf_op jit(solution)/shard_map/psum | solution.py:168
  136.4 1.8 slice_multiply_fusion
  138.2 1.7 div.26
  140.2 1.3 copy-done
  141.6 0.7 convert_reduce_fusion
  142.2 4.3 convolution_bitcast_fusion
  146.5 85.7 %all-gather.2.cloned.1.call-done.packed_hbm = f32[36,256,256]{2,1,0:T(8,128)} async-done(((f32[9,256,256]{2,1,0:T(8,128)}), f32[36,256,256]{2,1,0:T(8,128)}) %all-gather.2.cloned.1.call-update) | async-done | bytes 9437200 | tf_op jit(solution)/shard_map/all_gather | solution.py:171
  232.6 0.4 copy.22
  232.9 5.3 %pad_maximum_fusion = f32[2048,514]{1,0:T(8,128)} fusion(f32[2048,1]{1,0:T(8,128)S(1)} %copy.22, f32[2048,1]{1,0:T(8,128)S(1)} %copy.21, f32[2048,512]{1,0:T(8,128)} %convolution_bitcast_fusion), kind=kLoop, calls=%fused_computation.2 | loop fusion | flops 2105344 | bytes 8421376 | tf_op jit(solution)/shard_map/concatenate | solution.py:17
  238.3 201.0 %shard_map.37.l_hbm = f32[2048,2048]{1,0:T(8,128)} custom-call(f32[36,256,256]{2,1,0:T(8,128)} %all-gather.2.cloned.1.call-done.packed_hbm), custom_call_target="tpu_custom_call" | custom-call | tf_op jit(solution)/shard_map/pallas_call | solution.py:117
  439.3 1.0 fusion.15
  440.3 1.0 fusion.9
  441.3 13.9 %all_gather.7.c_ref = f32[64,2048]{1,0:T(8,128)S(1)} all-gather(f32[64,512]{1,0:T(8,128)S(1)} %fusion.9), channel_id=1, replica_groups=mesh['sample'=32,'protein'=4] {'protein'}, dimensions={1}, use_global_device_ids=true | all-gather | bytes 655360 | tf_op jit(solution)/shard_map/all_gather | solution.py:184
  455.2 19.3 %shard_map.38 = f32[64,2048]{1,0:T(8,128)S(1)} custom-call(f32[2048,2048]{1,0:T(8,128)} %shard_map.37.l_hbm, f32[64,2048]{1,0:T(8,128)S(1)} %all_gather.7.c_ref), custom_call_target="tpu_custom_call" | custom-call | tf_op jit(solution)/shard_map/pallas_call | solution.py:132
  474.5 0.7 constant_dynamic-slice_fusion
  (13 shorter events, 0.7 us)
Async XLA Ops:
  6.5 129.9 %all-reduce.2.cloned.1.call-start = ((), (), s32[]{:S(2)}) async-start(), calls=%async_computation.1 | async-start | bytes 4726784 | tf_op jit(solution)/shard_map/psum | solution.py:168
  26.0 206.2 %all-gather.2.cloned.1.call-start = ((), (), s32[]{:S(2)}) async-start(), calls=%async_computation.2 | async-start | bytes 11796480 | tf_op jit(solution)/shard_map/all_gather | solution.py:171
  140.0 1.6 copy-start
  140.0 299.3 %reduce-scatter.2.cloned.1.call-start = ((), (), s32[]{:S(2)}) async-start(), calls=%async_computation.3 | async-start | bytes 5406720 | tf_op jit(solution)/shard_map/reduce_scatter | solution.py:20
  238.3 202.1 %slice-start = ((f32[590336]{0:T(1024)}), f32[512]{0:T(512)S(1)}, s32[]{:S(2)}) async-start(f32[590336]{0:T(1024)} %all-reduce.2.cloned.1.call-done), calls=%async_computation.4 | async-start | bytes 4096 | tf_op jit(solution)/shard_map/slice | solution.py:170
Sparse Core Ops, SparseCore 0:
  26.1 110.2 all-reduce.1
  140.1 92.0 all-gather.1
  238.4 85.7 reduce-scatter.1
